TPU v7x, 512 devices: a whole 4x8x8 slice. The times are simulated.
512 devices in a mesh: section: 8 (over z), ctx: 8 (over y_hi, x), tp: 8 (over y_lo, core).
Axes of the slice: x: 4, y: 8 (y_hi: 2, y_lo: 4; y = y_hi * 4 + y_lo), z: 8, core: 2. Of those that a mesh axis runs over, the one named last changes fastest.
Arguments:
- block_order: int32 [16], replicated, may hold values from 0 to 15, each once
- plan: int32 [8], replicated, may hold values from 0 to 1
- q_box: bfloat16 [8, 2, 1408, 8192], P('section', None, 'ctx', 'tp'), may hold values from -8 to 8
- k_box: bfloat16 [8, 2, 1408, 1024], P('section', None, ('ctx', 'tp')), may hold values from -8 to 8
- v_box: bfloat16 [8, 2, 1408, 1024], P('section', None, ('ctx', 'tp')), may hold values from -6 to 6
- grad_out: bfloat16 [8, 1408, 8192], P('section', 'ctx', 'tp'), may hold values from -6 to 6
Outputs:
- attn_out: bfloat16 [8, 1408, 8192], P('section', 'ctx', 'tp')
- grad_q: bfloat16 [8, 1408, 8192], P('section', 'ctx', 'tp')
- grad_k: float32 [8, 1408, 1024], P('section', ('ctx', 'tp'))
- grad_v: float32 [8, 1408, 1024], P('section', ('ctx', 'tp'))
Inputs may be any that keep to these rules, and one draw needn't show every extreme that they name: `block_order`: a permutation: every block sits in exactly one storage slot, slot j covering storage rows j * 88 to (j + 1) * 88 - 1.
All inputs are finite; a program needn't handle non-finite values.
Results may differ from a plain program's by a relative error of at most 0.012.
Values may be sent and summed in bfloat16 or wider, within the bound.
No kernel may reach another device: no remote copies, remote signals or barrier semaphores. Data moves between devices by JAX's collectives and lax.ppermute only.
A program may use at most 64 MiB of HBM per device.

v0:
```python
import jax
import jax.numpy as jnp
from jax import lax
from jax.sharding import PartitionSpec as P

HEAD_DIM = 128
NEG = -1e30


def passed_along(block, axis, distance):
    devices = range(lax.axis_size(axis))
    route = [((i - distance) % len(devices), i) for i in devices]
    return lax.ppermute(block, axis, route)


def body(block_order, plan, q_box, k_box, v_box, grad_out):
    tp_count = lax.axis_size("tp")
    ctx_count = lax.axis_size("ctx")
    section_count = lax.axis_size("section")
    tok_rows = q_box.shape[2]
    kv_rows = k_box.shape[2]
    seq_rows = tok_rows * ctx_count
    block_len = seq_rows // block_order.shape[0]
    head_size = HEAD_DIM
    heads_local = q_box.shape[3] // head_size
    kv_local = k_box.shape[3] // head_size // tp_count
    group = heads_local // kv_local
    kv_width = kv_local * head_size
    scale = head_size ** (-0.5)
    section_rank = lax.axis_index("section")
    receiver = (section_rank + 1) % section_count
    wanted = lax.dynamic_index_in_dim(plan, receiver, 0, keepdims=False)

    def pick(box):
        slots = box[0]
        chosen = slots[0]
        for slot in range(1, slots.shape[0]):
            chosen = jnp.where(wanted == slot, slots[slot], chosen)
        return chosen

    q_send = pick(q_box)
    k_send = pick(k_box)
    v_send = pick(v_box)
    kv_send = jnp.stack(
        [k_send.reshape(kv_rows, -1, head_size), v_send.reshape(kv_rows, -1, head_size)], axis=2
    ).reshape(kv_rows, -1)
    queries, kv_rows_in = passed_along((q_send, kv_send), "section", 1)
    cotangent = passed_along(grad_out[0], "section", -1)
    plane = ("ctx", "tp")
    kv_pieces = kv_rows_in.reshape(1, kv_rows, tp_count, 2 * kv_width).transpose(0, 2, 1, 3)
    kv_pieces = jnp.broadcast_to(kv_pieces, (ctx_count, tp_count, kv_rows, 2 * kv_width))
    kv_pieces = kv_pieces.reshape(ctx_count * tp_count * kv_rows, 2 * kv_width)
    kv_full = lax.all_to_all(kv_pieces, plane, split_axis=0, concat_axis=0, tiled=True)
    kv_full = kv_full.reshape(seq_rows, kv_local, 2, head_size)
    key_heads = kv_full[:, :, 0, :]
    value_heads = kv_full[:, :, 1, :]
    ctx_rank = lax.axis_index("ctx")
    positions = (
        block_order[:, None] * block_len + jnp.arange(block_len, dtype=jnp.int32)[None, :]
    ).reshape(ctx_count, tok_rows)
    key_pos = positions.reshape(seq_rows)
    query_pos = lax.dynamic_index_in_dim(positions, ctx_rank, 0, keepdims=False)
    visible = (key_pos[None, :] <= query_pos[:, None])[None, None]
    q4 = queries.reshape(tok_rows, kv_local, group, head_size)
    do4 = cotangent.reshape(tok_rows, kv_local, group, head_size)
    scores = jnp.einsum("qgjd,kgd->gjqk", q4, key_heads, preferred_element_type=jnp.float32) * scale
    scores = jnp.where(visible, scores, NEG)
    top_score = jnp.max(scores, axis=-1, keepdims=True)
    totals = jnp.sum(jnp.exp(scores - top_score), axis=-1, keepdims=True)
    log_total = top_score + jnp.log(totals)
    probs = jnp.exp(scores - log_total)
    probs_low = probs.astype(jnp.bfloat16)
    attended = jnp.einsum(
        "gjqk,kgd->qgjd", probs_low, value_heads, preferred_element_type=jnp.float32
    )
    delta = jnp.sum(do4.astype(jnp.float32) * attended, axis=-1)
    dprobs = jnp.einsum("qgjd,kgd->gjqk", do4, value_heads, preferred_element_type=jnp.float32)
    dscores = (probs * (dprobs - jnp.transpose(delta, (1, 2, 0))[..., None])).astype(jnp.bfloat16)
    q_grad = (
        jnp.einsum("gjqk,kgd->qgjd", dscores, key_heads, preferred_element_type=jnp.float32) * scale
    ).astype(jnp.bfloat16)
    key_grad = jnp.einsum("gjqk,qgjd->kgd", dscores, q4, preferred_element_type=jnp.float32) * scale
    value_grad = jnp.einsum("gjqk,qgjd->kgd", probs_low, do4, preferred_element_type=jnp.float32)
    attended_flat = attended.astype(jnp.bfloat16).reshape(tok_rows, heads_local * head_size)
    q_grad_flat = q_grad.reshape(tok_rows, heads_local * head_size)
    grad_terms = jnp.stack([key_grad, value_grad], axis=2).reshape(seq_rows, 2 * kv_width)
    grad_parts = lax.all_to_all(
        grad_terms.astype(jnp.bfloat16), plane, split_axis=0, concat_axis=1, tiled=True
    )
    grad_parts = grad_parts.reshape(kv_rows, ctx_count, tp_count * kv_local, 2, head_size)
    own_grads = jnp.sum(grad_parts.astype(jnp.float32), axis=1)
    k_grad_tokens = own_grads[:, :, 0, :].reshape(kv_rows, -1)
    v_grad_tokens = own_grads[:, :, 1, :].reshape(kv_rows, -1)
    return (attended_flat[None], q_grad_flat[None], k_grad_tokens[None], v_grad_tokens[None])


def solution(mesh):
    in_specs = (
        P(),
        P(),
        P("section", None, "ctx", "tp"),
        P("section", None, ("ctx", "tp"), None),
        P("section", None, ("ctx", "tp"), None),
        P("section", "ctx", "tp"),
    )
    out_specs = (
        P("section", "ctx", "tp"),
        P("section", "ctx", "tp"),
        P("section", ("ctx", "tp"), None),
        P("section", ("ctx", "tp"), None),
    )
    return jax.shard_map(body, mesh=mesh, in_specs=in_specs, out_specs=out_specs, check_vma=False)
```

profile of v0, /device:TPU:1, one launch (start us, length us, event | category | flops | bytes accessed | tf_op | source)
XLA Modules:
  0.0 97.7 jit_solution(3275048713458376290)
XLA Ops:
  0.6 1.2 %dynamic_slice.8 = s32[1]{0:T(128)} dynamic-slice(s32[8]{0:T(128)} %param.7, s32[]{:T(128)S(6)} %select_n.63), dynamic_slice_sizes={1} | dynamic-slice | bytes 12 | tf_op jit(solution)/shard_map/jit(dynamic_index_in_dim)/dynamic_slice | solution.py:32
  2.5 1.6 %fusion.32 = (bf16[22,1024]{1,0:T(8,128)(2,1)S(1)}, bf16[22,1024]{1,0:T(8,128)(2,1)S(1)}) fusion(pred[]{:T(512)} %bitcast, bf16[1,2,22,1024]{3,1,2,0:T(2,128)(2,1)} %param.9, bf16[1,2,22,1024]{3,1,2,0:T(2,128)(2,1)} %param.10), kind=kLoop, calls=%fused_computation.40 | loop fusion | flops 45056 | bytes 270337 | tf_op jit(solution)/shard_map/jit(_where)/select_n | solution.py:38
  4.3 4.8 %collective-permute-start = (bf16[22,2048]{1,0:T(8,128)(2,1)S(1)}, bf16[22,2048]{1,0:T(8,128)(2,1)S(1)}, u32[]{:S(2)}, u32[]{:S(2)}) collective-permute-start(bf16[22,2048]{1,0:T(8,128)(2,1)S(1)} %reshape.224), channel_id=1, source_target_pairs={{448,0},{0,64},{64,128},{128,192},{192,256},{256,320},{320,384},{3... | collective-permute-start | bytes 270344 | tf_op jit(solution)/shard_map/ppermute | solution.py:13
  9.1 8.6 %collective-permute-start.2 = (bf16[176,1024]{1,0:T(8,128)(2,1)}, bf16[176,1024]{1,0:T(8,128)(2,1)S(1)}, u32[]{:S(2)}, u32[]{:S(2)}) collective-permute-start(bf16[176,1024]{1,0:T(8,128)(2,1)} %bitcast.165), channel_id=1, source_target_pairs={{64,0},{128,64},{192,128},{256,192},{320,256},{384,320},{448,384},... | collective-permute-start | bytes 1081352 | tf_op jit(solution)/shard_map/ppermute | solution.py:13
  17.7 0.6 collective-permute-done
  18.4 0.9 broadcast_in_dim.17
  19.3 11.4 %all-to-all-start = ((bf16[64,22,256]{2,1,0:T(8,128)(2,1)}), bf16[64,22,256]{2,1,0:T(8,128)(2,1)S(1)}, u32[]{:S(2)}, u32[]{:S(2)}) async-start(bf16[64,22,256]{2,1,0:T(8,128)(2,1)} %bitcast.3), calls=%async_computation | async-start | bytes 1572864 | tf_op jit(solution)/shard_map/all_to_all | solution.py:53
  30.7 1.1 %select_bitcast_fusion = bf16[176,1024]{1,0:T(8,128)(2,1)S(1)} fusion(bf16[1,2,176,1024]{3,2,1,0:T(8,128)(2,1)} %param.8, pred[]{:T(512)} %bitcast), kind=kLoop, calls=%fused_computation.35 | loop fusion | flops 180224 | bytes 1081345 | tf_op jit(solution)/shard_map/jit(_where)/select_n | solution.py:38
  31.8 1.9 %collective-permute-start.1 = (bf16[176,1024]{1,0:T(8,128)(2,1)S(1)}, bf16[176,1024]{1,0:T(8,128)(2,1)S(1)}, u32[]{:S(2)}, u32[]{:S(2)}) collective-permute-start(bf16[176,1024]{1,0:T(8,128)(2,1)S(1)} %select_bitcast_fusion), channel_id=1, source_target_pairs={{448,0},{0,64},{64,128},{128,192},{192,256},{256,320},{320,384},{3... | collective-permute-start | bytes 1081352 | tf_op jit(solution)/shard_map/ppermute | solution.py:13
  33.7 0.7 broadcast_multiply_fusion
  34.9 0.2 broadcast_compare_fusion
  35.2 0.1 copy.78
  35.3 9.1 %collective-permute-done.1 = bf16[176,1024]{1,0:T(8,128)(2,1)S(1)} collective-permute-done((bf16[176,1024]{1,0:T(8,128)(2,1)S(1)}, bf16[176,1024]{1,0:T(8,128)(2,1)S(1)}, u32[]{:S(2)}, u32[]{:S(2)}) %collective-permute-start.1) | collective-permute-done | bytes 360480 | tf_op jit(solution)/shard_map/ppermute | solution.py:13
  44.4 0.8 copy.79
  45.2 9.2 %all-to-all-done = bf16[64,22,256]{2,1,0:T(8,128)(2,1)S(1)} async-done(((bf16[64,22,256]{2,1,0:T(8,128)(2,1)}), bf16[64,22,256]{2,1,0:T(8,128)(2,1)S(1)}, u32[]{:S(2)}, u32[]{:S(2)}) %all-to-all-start) | async-done | bytes 720928 | tf_op jit(solution)/shard_map/all_to_all | solution.py:53
  54.5 0.3 reshape.226
  54.8 1.1 %fusion.34 = (bf16[1408,1,1,128]{3,2,0,1:T(2,128)(2,1)S(1)}, bf16[1408,1,1,128]{3,2,0,1:T(2,128)(2,1)S(1)}) fusion(bf16[1408,1,2,128]{3,2,0,1:T(2,128)(2,1)S(1)} %reshape.226), kind=kLoop, calls=%fused_computation.50 | loop fusion | bytes 1441792 | tf_op jit(solution)/shard_map/slice | solution.py:56
  55.8 1.9 %fusion.36 = (f32[8,176]{1,0:T(8,128)S(1)}, f32[1,8,176,1408]{3,2,1,0:T(8,128)S(1)}) fusion(bf16[1408,1,1,128]{3,2,0,1:T(2,128)(2,1)S(1)} %get-tuple-element.11, pred[176,1408]{1,0:T(8,128)(4,1)S(1)} %broadcast_compare_fusion, bf16[176,1024]{1,0:T(8,128)(2,1)S(1)} %collective-permute-done.1), kind=kOutput, calls=%fused_computation.52 | convolution fusion | flops 513456768 | bytes 8904192 | tf_op jit(solution)/shard_map/qgjd,kgd->gjqk/dot_general | solution.py:66
  57.7 1.2 %exponential_reduce_fusion = f32[8,176]{1,0:T(8,128)S(1)} fusion(f32[1,8,176,1408]{3,2,1,0:T(8,128)S(1)} %get-tuple-element.15, f32[8,176]{1,0:T(8,128)S(1)} %get-tuple-element.14), kind=kLoop, calls=%fused_computation.5 | loop fusion | flops 3963520 | bytes 7941120 | tf_op jit(solution)/shard_map/reduce_sum | solution.py:69
  59.0 1.7 %fusion.25 = (f32[176,8]{0,1:T(8,128)S(1)}, bf16[176,1,8,128]{3,0,2,1:T(8,128)(2,1)S(1)}) fusion(f32[176,1,8,128]{3,2,0,1:T(8,128)S(1)} %bitcast.152, f32[1,8,176,1408]{3,2,1,0:T(8,128)S(1)} %get-tuple-element.15, f32[8,176]{1,0:T(8,128)S(1)} %log_add_fusion, bf16[1408,1,1,128]{3,2,0,1:T(2,128)(2,1)S(1)} %get-tuple-element.10), kind=kOutput, calls=%fused_computation.26 | convolution fusion | flops 512014976 | bytes 9382912 | tf_op jit(solution)/shard_map/gjqk,kgd->qgjd/dot_general | solution.py:73
  60.7 2.2 %fusion.6 = bf16[8,176,1408]{2,1,0:T(8,128)(2,1)S(1)} fusion(f32[8,176]{1,0:T(8,128)S(1)} %bitcast.163, f32[1,8,176,1408]{3,2,1,0:T(8,128)S(1)} %get-tuple-element.15, f32[8,176]{1,0:T(8,128)S(1)} %log_add_fusion, bf16[1408,1,1,128]{3,2,0,1:T(2,128)(2,1)S(1)} %get-tuple-element.10, bf16[176,1024]{1,0:T(8,128)(2,1)S(1)} %collective-permute-done.2), kind=kOutput, calls=%fused_computation.10 | convolution fusion | flops 515440640 | bytes 12626944 | tf_op jit(solution)/shard_map/qgjd,kgd->gjqk/dot_general | solution.py:77
  62.9 0.9 fusion.17
  63.8 1.5 %fusion.20 = bf16[1408,1,1,128]{0,3,2,1:T(8,128)(2,1)S(1)} fusion(f32[1,8,176,1408]{3,2,1,0:T(8,128)S(1)} %get-tuple-element.15, f32[8,176]{1,0:T(8,128)S(1)} %log_add_fusion, bf16[176,1024]{1,0:T(8,128)(2,1)S(1)} %collective-permute-done.2), kind=kOutput, calls=%fused_computation.17 | convolution fusion | flops 511655936 | bytes 8656384 | tf_op jit(solution)/shard_map/gjqk,qgjd->kgd/dot_general | solution.py:83
  65.4 1.0 %copy.67 = bf16[1408,1,2,128]{3,2,0,1:T(2,128)(2,1)S(1)} copy(bf16[1408,1,2,128]{0,3,2,1:T(8,128)(2,1)S(1)} %pad_maximum_fusion) | data formatting | bytes 1441792 | tf_op jit(solution)/shard_map/stack | solution.py:86
  66.5 1.3 %convert_element_type.54 = bf16[64,22,256]{2,1,0:T(8,128)(2,1)} reshape(bf16[1408,1,2,128]{3,2,0,1:T(2,128)(2,1)S(1)} %copy.67) | data formatting | bytes 1441792 | tf_op jit(solution)/shard_map/convert_element_type | solution.py:88
  67.8 4.9 %all-to-all-start.1 = ((bf16[64,22,256]{2,1,0:T(8,128)(2,1)}), bf16[64,22,256]{2,1,0:T(8,128)(2,1)S(1)}, u32[]{:S(2)}, u32[]{:S(2)}) async-start(bf16[64,22,256]{2,1,0:T(8,128)(2,1)} %convert_element_type.54), calls=%async_computation.1 | async-start | bytes 1572864 | tf_op jit(solution)/shard_map/all_to_all | solution.py:87
  72.8 0.9 broadcast_in_dim_reshape.6
  73.7 3.3 %fusion.22 = bf16[176,1,8,128]{3,0,2,1:T(8,128)(2,1)S(1)} fusion(bf16[8,176,1408]{2,1,0:T(8,128)(2,1)} %copy-done, bf16[1408,1,1,128]{3,2,0,1:T(2,128)(2,1)S(1)} %get-tuple-element.11), kind=kOutput, calls=%fused_computation.23 | convolution fusion | flops 507871232 | bytes 4685824 | tf_op jit(solution)/shard_map/gjqk,kgd->qgjd/dot_general | solution.py:80
  77.1 0.9 broadcast_in_dim_reshape.7
  78.0 18.5 %all-to-all-done.1 = bf16[64,22,256]{2,1,0:T(8,128)(2,1)S(1)} async-done(((bf16[64,22,256]{2,1,0:T(8,128)(2,1)}), bf16[64,22,256]{2,1,0:T(8,128)(2,1)S(1)}, u32[]{:S(2)}, u32[]{:S(2)}) %all-to-all-start.1) | async-done | bytes 720928 | tf_op jit(solution)/shard_map/all_to_all | solution.py:87
  96.7 0.4 bitcast_reduce_fusion
  97.1 0.7 fusion.35
  (29 shorter events, 1.2 us)
Async XLA Ops:
  4.3 14.0 %collective-permute-start = (bf16[22,2048]{1,0:T(8,128)(2,1)S(1)}, bf16[22,2048]{1,0:T(8,128)(2,1)S(1)}, u32[]{:S(2)}, u32[]{:S(2)}) collective-permute-start(bf16[22,2048]{1,0:T(8,128)(2,1)S(1)} %reshape.224), channel_id=1, source_target_pairs={{448,0},{0,64},{64,128},{128,192},{192,256},{256,320},{320,384},{3... | collective-permute-start | bytes 270344 | tf_op jit(solution)/shard_map/ppermute | solution.py:13
  9.1 26.0 %collective-permute-start.2 = (bf16[176,1024]{1,0:T(8,128)(2,1)}, bf16[176,1024]{1,0:T(8,128)(2,1)S(1)}, u32[]{:S(2)}, u32[]{:S(2)}) collective-permute-start(bf16[176,1024]{1,0:T(8,128)(2,1)} %bitcast.165), channel_id=1, source_target_pairs={{64,0},{128,64},{192,128},{256,192},{320,256},{384,320},{448,384},... | collective-permute-start | bytes 1081352 | tf_op jit(solution)/shard_map/ppermute | solution.py:13
  19.3 35.2 %all-to-all-start = ((bf16[64,22,256]{2,1,0:T(8,128)(2,1)}), bf16[64,22,256]{2,1,0:T(8,128)(2,1)S(1)}, u32[]{:S(2)}, u32[]{:S(2)}) async-start(bf16[64,22,256]{2,1,0:T(8,128)(2,1)} %bitcast.3), calls=%async_computation | async-start | bytes 1572864 | tf_op jit(solution)/shard_map/all_to_all | solution.py:53
  31.8 12.6 %collective-permute-start.1 = (bf16[176,1024]{1,0:T(8,128)(2,1)S(1)}, bf16[176,1024]{1,0:T(8,128)(2,1)S(1)}, u32[]{:S(2)}, u32[]{:S(2)}) collective-permute-start(bf16[176,1024]{1,0:T(8,128)(2,1)S(1)} %select_bitcast_fusion), channel_id=1, source_target_pairs={{448,0},{0,64},{64,128},{128,192},{192,256},{256,320},{320,384},{3... | collective-permute-start | bytes 1081352 | tf_op jit(solution)/shard_map/ppermute | solution.py:13
  60.7 2.2 %copy-start.1 = (bf16[22,8,8,128]{3,2,1,0:T(8,128)(2,1)S(1)}, bf16[22,8,8,128]{3,2,1,0:T(8,128)(2,1)}, u32[]{:S(2)}) copy-start(bf16[22,8,8,128]{3,2,1,0:T(8,128)(2,1)} %copy.79) | copy-start | bytes 1081348
  62.9 2.4 %copy-start = (bf16[8,176,1408]{2,1,0:T(8,128)(2,1)}, bf16[8,176,1408]{2,1,0:T(8,128)(2,1)S(1)}, u32[]{:S(2)}) copy-start(bf16[8,176,1408]{2,1,0:T(8,128)(2,1)S(1)} %fusion.6) | copy-start | bytes 11894788
  67.8 28.7 %all-to-all-start.1 = ((bf16[64,22,256]{2,1,0:T(8,128)(2,1)}), bf16[64,22,256]{2,1,0:T(8,128)(2,1)S(1)}, u32[]{:S(2)}, u32[]{:S(2)}) async-start(bf16[64,22,256]{2,1,0:T(8,128)(2,1)} %convert_element_type.54), calls=%async_computation.1 | async-start | bytes 1572864 | tf_op jit(solution)/shard_map/all_to_all | solution.py:87
where the time goes:
time: 98.2 us; the launch traced here: 97.7 us
  waiting for transfers between devices  37.4 us (38%)
  starting transfers between devices  31.6 us (32%)
  matrix products  11.5 us (12%)
  local copies, waits for them, and re-layouts  10.1 us (10%)
  other arithmetic  5.55 us (6%)
  between operations  1.6 us (2%)
    all_to_all x1, waiting for transfers between devices, body(): lax.all_to_all(grad_terms.astype(jnp.bfloat16), plane, split_axis=0, conc...  18.5 us
    ppermute x3, starting transfers between devices, passed_along(): return lax.ppermute(block, axis, route)  15.3 us
    all_to_all x1, starting transfers between devices, body(): lax.all_to_all(kv_pieces, plane, split_axis=0, concat_axis=0, tiled=True)  11.4 us
    ppermute x3, waiting for transfers between devices, passed_along(): return lax.ppermute(block, axis, route)  9.64 us
    all_to_all x1, waiting for transfers between devices, body(): lax.all_to_all(kv_pieces, plane, split_axis=0, concat_axis=0, tiled=True)  9.24 us
    all_to_all x1, starting transfers between devices, body(): lax.all_to_all(grad_terms.astype(jnp.bfloat16), plane, split_axis=0, conc...  4.92 us
    dot_general x1, matrix products, body(): jnp.einsum('gjqk,kgd->qgjd', dscores, key_heads, preferred_element_type=j...  3.31 us
    select_n x2, other arithmetic, pick(): chosen = jnp.where(wanted == slot, slots[slot], chosen)  2.7 us
  transfers between devices with their start and end apart: 5, of which 4 were waited for; matrix products, arithmetic and copies ran while one was open for 10% of the time, Pallas kernels for 0%

commit v1 on v0

--- a/solution.py
+++ b/solution.py
@@ -84,8 +84,14 @@
     attended_flat = attended.astype(jnp.bfloat16).reshape(tok_rows, heads_local * head_size)
     q_grad_flat = q_grad.reshape(tok_rows, heads_local * head_size)
     grad_terms = jnp.stack([key_grad, value_grad], axis=2).reshape(seq_rows, 2 * kv_width)
-    grad_parts = lax.all_to_all(
-        grad_terms.astype(jnp.bfloat16), plane, split_axis=0, concat_axis=1, tiled=True
+    grad_parts = jnp.concatenate(
+        lax.all_to_all(
+            jnp.stack(jnp.split(grad_terms.astype(jnp.bfloat16), lax.axis_size(plane), axis=0)),
+            plane,
+            0,
+            0,
+        ),
+        axis=1,
     )
     grad_parts = grad_parts.reshape(kv_rows, ctx_count, tp_count * kv_local, 2, head_size)
     own_grads = jnp.sum(grad_parts.astype(jnp.float32), axis=1)

time: 98.2 us -> 205 us (2.09); the launches traced: 97.7 us -> 202 us
  local copies, waits for them, and re-layouts: 10.1 us -> 110 us
  other arithmetic: 5.55 us -> 9.72 us
    unnamed x9 -> x76, local copies, waits for them, and re-layouts: 0.99 us -> 59.2 us
    another operation x1 -> x65, local copies, waits for them, and re-layouts: 1.04 us -> 45.1 us  [body(): jnp.stack(jnp.split(grad_terms.astype(jnp.bfloat16), lax.axis_size(plane)...]
    another operation x1 -> x8, other arithmetic: 0.08 us -> 4.66 us  [body(): jnp.stack([key_grad, value_grad], axis=2).reshape(seq_rows, 2 * kv_width)]
  transfers between devices with their start and end apart: 5 -> 5, of which waited for: 4 -> 4; matrix products, arithmetic and copies ran while one was open for 10% -> 5% of each run, Pallas kernels for 0% -> 0%
where the time goes in v1:
time: 205 us; the launch traced here: 202 us
  local copies, waits for them, and re-layouts  110 us (54%)
  waiting for transfers between devices  37.4 us (18%)
  starting transfers between devices  31.6 us (15%)
  matrix products  11.7 us (6%)
  other arithmetic  9.72 us (5%)
    unnamed x76, local copies, waits for them, and re-layouts  59.2 us
    another operation x65, local copies, waits for them, and re-layouts, body(): jnp.stack(jnp.split(grad_terms.astype(jnp.bfloat16), lax.axis_size(plane)...  45.1 us
    all_to_all x1, waiting for transfers between devices, body(): lax.all_to_all(jnp.stack(jnp.split(grad_terms.astype(jnp.bfloat16), lax.a...  18.5 us
    ppermute x3, starting transfers between devices, passed_along(): return lax.ppermute(block, axis, route)  15.3 us
    all_to_all x1, starting transfers between devices, body(): lax.all_to_all(kv_pieces, plane, split_axis=0, concat_axis=0, tiled=True)  11.4 us
    ppermute x3, waiting for transfers between devices, passed_along(): return lax.ppermute(block, axis, route)  9.64 us
    all_to_all x1, waiting for transfers between devices, body(): lax.all_to_all(kv_pieces, plane, split_axis=0, concat_axis=0, tiled=True)  9.24 us
    all_to_all x1, starting transfers between devices, body(): lax.all_to_all(jnp.stack(jnp.split(grad_terms.astype(jnp.bfloat16), lax.a...  4.93 us
  transfers between devices with their start and end apart: 5, of which 4 were waited for; matrix products, arithmetic and copies ran while one was open for 5% of the time, Pallas kernels for 0%

profile of v1, /device:TPU:1, one launch (start us, length us, event | category | flops | bytes accessed | tf_op | source)
XLA Modules:
  0.0 202.5 jit_solution(9806546365954500626)
XLA Ops:
  2.5 1.6 fusion.32
  4.3 4.8 %collective-permute-start = (bf16[22,2048]{1,0:T(8,128)(2,1)S(1)}, bf16[22,2048]{1,0:T(8,128)(2,1)S(1)}, u32[]{:S(2)}, u32[]{:S(2)}) collective-permute-start(bf16[22,2048]{1,0:T(8,128)(2,1)S(1)} %reshape.347), channel_id=1, source_target_pairs={{448,0},{0,64},{64,128},{128,192},{192,256},{256,320},{320,384},{3... | collective-permute-start | bytes 270344 | tf_op jit(solution)/shard_map/ppermute | solution.py:13
  9.1 8.6 %collective-permute-start.2 = (bf16[176,1024]{1,0:T(8,128)(2,1)}, bf16[176,1024]{1,0:T(8,128)(2,1)S(1)}, u32[]{:S(2)}, u32[]{:S(2)}) collective-permute-start(bf16[176,1024]{1,0:T(8,128)(2,1)} %bitcast.291), channel_id=1, source_target_pairs={{64,0},{128,64},{192,128},{256,192},{320,256},{384,320},{448,384},... | collective-permute-start | bytes 1081352 | tf_op jit(solution)/shard_map/ppermute | solution.py:13
  19.3 11.4 %all-to-all-start = ((bf16[64,22,256]{2,1,0:T(8,128)(2,1)}), bf16[64,22,256]{2,1,0:T(8,128)(2,1)S(1)}, u32[]{:S(2)}, u32[]{:S(2)}) async-start(bf16[64,22,256]{2,1,0:T(8,128)(2,1)} %bitcast.3), calls=%async_computation | async-start | bytes 1572864 | tf_op jit(solution)/shard_map/all_to_all | solution.py:53
  31.8 1.9 collective-permute-start.1
  35.4 9.1 %collective-permute-done.1 = bf16[176,1024]{1,0:T(8,128)(2,1)S(1)} collective-permute-done((bf16[176,1024]{1,0:T(8,128)(2,1)S(1)}, bf16[176,1024]{1,0:T(8,128)(2,1)S(1)}, u32[]{:S(2)}, u32[]{:S(2)}) %collective-permute-start.1) | collective-permute-done | bytes 360480 | tf_op jit(solution)/shard_map/ppermute | solution.py:13
  45.2 9.2 %all-to-all-done = bf16[64,22,256]{2,1,0:T(8,128)(2,1)S(1)} async-done(((bf16[64,22,256]{2,1,0:T(8,128)(2,1)}), bf16[64,22,256]{2,1,0:T(8,128)(2,1)S(1)}, u32[]{:S(2)}, u32[]{:S(2)}) %all-to-all-start) | async-done | bytes 720928 | tf_op jit(solution)/shard_map/all_to_all | solution.py:53
  55.8 1.9 fusion.99
  59.0 1.7 fusion.25
  60.7 2.4 %fusion.6 = bf16[8,176,1408]{2,1,0:T(8,128)(2,1)S(1)} fusion(f32[8,176]{1,0:T(8,128)S(1)} %bitcast.289, f32[1,8,176,1408]{3,2,1,0:T(8,128)S(1)} %get-tuple-element.86, f32[8,176]{1,0:T(8,128)S(1)} %log_add_fusion, bf16[1408,1,1,128]{3,2,0,1:T(2,128)(2,1)S(1)} %get-tuple-element.81, bf16[176,1024]{1,0:T(8,128)(2,1)S(1)} %collective-permute-done.2), kind=kOutput, calls=%fused_computation.136 | convolution fusion | flops 515440640 | bytes 12626944 | tf_op jit(solution)/shard_map/qgjd,kgd->gjqk/dot_general | solution.py:77
  71.8 1.5 copy.198
  73.3 1.5 copy.199
  74.8 1.5 copy.200
  76.4 1.5 copy.201
  79.4 1.5 copy.203
  85.5 1.5 copy.207
  87.1 1.5 copy.208
  88.6 1.5 copy.209
  90.1 1.5 copy.210
  91.7 1.5 copy.211
  93.2 1.5 copy.212
  96.2 1.5 copy.214
  99.3 1.5 copy.216
  100.8 1.5 copy.217
  103.9 1.5 copy.219
  105.4 1.5 copy.220
  107.0 1.5 copy.221
  108.5 1.5 copy.222
  110.0 1.5 copy.223
  171.5 4.9 %all-to-all-start.1 = ((bf16[64,22,256]{2,1,0:T(8,128)(2,1)}), bf16[64,22,256]{2,1,0:T(8,128)(2,1)S(1)}, u32[]{:S(2)}, u32[]{:S(2)}) async-start(bf16[64,22,256]{2,1,0:T(8,128)(2,1)} %constant_dynamic-update-slice_fusion), calls=%async_computation.1 | async-start | bytes 1572864 | tf_op jit(solution)/shard_map/all_to_all | solution.py:88
  177.4 3.3 %fusion.22 = bf16[176,1,8,128]{3,0,2,1:T(8,128)(2,1)S(1)} fusion(bf16[8,176,1408]{2,1,0:T(8,128)(2,1)} %copy-done, bf16[1408,1,1,128]{3,2,0,1:T(2,128)(2,1)S(1)} %get-tuple-element.82), kind=kOutput, calls=%fused_computation.148 | convolution fusion | flops 507871232 | bytes 4685824 | tf_op jit(solution)/shard_map/gjqk,kgd->qgjd/dot_general | solution.py:80
  181.7 18.5 %all-to-all-done.1 = bf16[64,22,256]{2,1,0:T(8,128)(2,1)S(1)} async-done(((bf16[64,22,256]{2,1,0:T(8,128)(2,1)}), bf16[64,22,256]{2,1,0:T(8,128)(2,1)S(1)}, u32[]{:S(2)}, u32[]{:S(2)}) %all-to-all-start.1) | async-done | bytes 720928 | tf_op jit(solution)/shard_map/all_to_all | solution.py:88
  (165 shorter events, 92.3 us)
Async XLA Ops:
  4.3 14.0 %collective-permute-start = (bf16[22,2048]{1,0:T(8,128)(2,1)S(1)}, bf16[22,2048]{1,0:T(8,128)(2,1)S(1)}, u32[]{:S(2)}, u32[]{:S(2)}) collective-permute-start(bf16[22,2048]{1,0:T(8,128)(2,1)S(1)} %reshape.347), channel_id=1, source_target_pairs={{448,0},{0,64},{64,128},{128,192},{192,256},{256,320},{320,384},{3... | collective-permute-start | bytes 270344 | tf_op jit(solution)/shard_map/ppermute | solution.py:13
  9.1 26.0 %collective-permute-start.2 = (bf16[176,1024]{1,0:T(8,128)(2,1)}, bf16[176,1024]{1,0:T(8,128)(2,1)S(1)}, u32[]{:S(2)}, u32[]{:S(2)}) collective-permute-start(bf16[176,1024]{1,0:T(8,128)(2,1)} %bitcast.291), channel_id=1, source_target_pairs={{64,0},{128,64},{192,128},{256,192},{320,256},{384,320},{448,384},... | collective-permute-start | bytes 1081352 | tf_op jit(solution)/shard_map/ppermute | solution.py:13
  19.3 35.2 %all-to-all-start = ((bf16[64,22,256]{2,1,0:T(8,128)(2,1)}), bf16[64,22,256]{2,1,0:T(8,128)(2,1)S(1)}, u32[]{:S(2)}, u32[]{:S(2)}) async-start(bf16[64,22,256]{2,1,0:T(8,128)(2,1)} %bitcast.3), calls=%async_computation | async-start | bytes 1572864 | tf_op jit(solution)/shard_map/all_to_all | solution.py:53
  31.8 12.6 %collective-permute-start.1 = (bf16[176,1024]{1,0:T(8,128)(2,1)S(1)}, bf16[176,1024]{1,0:T(8,128)(2,1)S(1)}, u32[]{:S(2)}, u32[]{:S(2)}) collective-permute-start(bf16[176,1024]{1,0:T(8,128)(2,1)S(1)} %select_bitcast_fusion), channel_id=1, source_target_pairs={{448,0},{0,64},{64,128},{128,192},{192,256},{256,320},{320,384},{3... | collective-permute-start | bytes 1081352 | tf_op jit(solution)/shard_map/ppermute | solution.py:13
  60.7 2.4 %copy-start.1 = (bf16[22,8,8,128]{3,2,1,0:T(8,128)(2,1)S(1)}, bf16[22,8,8,128]{3,2,1,0:T(8,128)(2,1)}, u32[]{:S(2)}) copy-start(bf16[22,8,8,128]{3,2,1,0:T(8,128)(2,1)} %copy.278) | copy-start | bytes 1081348
  63.1 2.4 %copy-start = (bf16[8,176,1408]{2,1,0:T(8,128)(2,1)}, bf16[8,176,1408]{2,1,0:T(8,128)(2,1)S(1)}, u32[]{:S(2)}) copy-start(bf16[8,176,1408]{2,1,0:T(8,128)(2,1)S(1)} %fusion.6) | copy-start | bytes 11894788
  171.5 28.7 %all-to-all-start.1 = ((bf16[64,22,256]{2,1,0:T(8,128)(2,1)}), bf16[64,22,256]{2,1,0:T(8,128)(2,1)S(1)}, u32[]{:S(2)}, u32[]{:S(2)}) async-start(bf16[64,22,256]{2,1,0:T(8,128)(2,1)} %constant_dynamic-update-slice_fusion), calls=%async_computation.1 | async-start | bytes 1572864 | tf_op jit(solution)/shard_map/all_to_all | solution.py:88
